TPU v7x, 256 devices: a whole 4x4x8 slice. The times are simulated.
256 devices in a mesh: expert: 16 (over z, core), fsdp: 16 (over x, y).
Axes of the slice: x: 4, y: 4, z: 8, core: 2. Of those that a mesh axis runs over, the one named last changes fastest.
Arguments:
- tokens: bfloat16 [4096, 6144], P(('expert', 'fsdp')), may hold values from -6 to 6
- expert_ids: int32 [4096, 4], P(('expert', 'fsdp')), may hold values from 0 to 15, all different within a row; in each aligned block of 16 rows (0 to 15, 16 to 31, ...) at most 5 rows name the same one
- router_weight: float32 [4096, 4], P(('expert', 'fsdp')), may hold values from 0.1 to 1
- w_gate: bfloat16 [16, 5376, 6144], P('expert', 'fsdp'), may hold values from -0.078125 to 0.078125
- w_up: bfloat16 [16, 5376, 6144], P('expert', 'fsdp'), may hold values from -0.078125 to 0.078125
Outputs:
- routed: bfloat16 [4096, 4, 5376], P(('expert', 'fsdp'))
Inputs may be any that keep to these rules, and one draw needn't show every extreme that they name: `expert_ids`: each row names 4 different experts; the 16 rows of one device name any one expert at most 5 times, and some device names some expert exactly 5 times.
All inputs are finite; a program needn't handle non-finite values.
Results may differ from a plain program's by a relative error of at most 0.0049.
Values may be sent and summed in bfloat16 or wider, within the bound.
No kernel may reach another device: no remote copies, remote signals or barrier semaphores. Data moves between devices by JAX's collectives and lax.ppermute only.
A program may use at most 128 MiB of HBM per device.

v0:
```python
import jax
import jax.numpy as jnp
from jax import lax
from jax.sharding import PartitionSpec as P


def hidden_block(row_block, gate_rows, up_rows):
    gate_act = lax.dot_general(
        row_block, gate_rows, (((1,), (1,)), ((), ())), preferred_element_type=jnp.float32
    )
    up_act = lax.dot_general(
        row_block, up_rows, (((1,), (1,)), ((), ())), preferred_element_type=jnp.float32
    )
    return (jax.nn.gelu(gate_act, approximate=False) * up_act).astype(jnp.bfloat16)


def local(tokens, expert_ids, router_weight, w_gate, w_up):
    tok_rows, model_width = tokens.shape
    top_count = expert_ids.shape[1]
    experts = lax.axis_size("expert")
    fsdp_size = lax.axis_size("fsdp")
    cap_slots = 5 * tok_rows * top_count // (4 * experts)
    flat_ids = expert_ids.reshape(-1)
    choosing = (flat_ids[:, None] == jnp.arange(experts, dtype=jnp.int32)[None, :]).astype(
        jnp.int32
    )
    slot_rank = jnp.sum((jnp.cumsum(choosing, axis=0) - 1) * choosing, axis=1)
    slot_of = flat_ids * cap_slots + slot_rank
    placing = (
        slot_of[None, :] == jnp.arange(experts * cap_slots, dtype=jnp.int32)[:, None]
    ).astype(jnp.bfloat16)
    repeated = jnp.repeat(tokens, top_count, axis=0)
    outgoing = jnp.dot(placing, repeated, preferred_element_type=jnp.float32).astype(jnp.bfloat16)
    outgoing = outgoing.reshape(experts, cap_slots, model_width)
    gate_rows = w_gate[0]
    up_rows = w_up[0]
    columns = gate_rows.shape[0]
    arrived = lax.all_to_all(outgoing, "expert", split_axis=0, concat_axis=0, tiled=True)
    local_hidden = hidden_block(
        lax.all_gather(arrived.reshape(-1, model_width), "fsdp", axis=0, tiled=True),
        gate_rows,
        up_rows,
    )
    shaped = local_hidden.reshape(fsdp_size, experts, cap_slots, columns)
    step_one = lax.all_to_all(shaped, "expert", split_axis=1, concat_axis=1, tiled=True)
    returned = lax.all_to_all(step_one, "fsdp", split_axis=0, concat_axis=3, tiled=True)
    returned = returned.reshape(experts * cap_slots, -1)
    collected = lax.dot_general(
        placing, returned, (((0,), (0,)), ((), ())), preferred_element_type=jnp.float32
    )
    routed = (router_weight.reshape(-1, 1) * collected).astype(jnp.bfloat16)
    return routed.reshape(tok_rows, top_count, -1)


def solution(mesh):
    return jax.shard_map(
        local,
        mesh=mesh,
        in_specs=(
            P(("expert", "fsdp"), None),
            P(("expert", "fsdp"), None),
            P(("expert", "fsdp"), None),
            P("expert", "fsdp", None),
            P("expert", "fsdp", None),
        ),
        out_specs=P(("expert", "fsdp"), None, None),
        check_vma=False,
    )
```

profile of v0, /device:TPU:1, one launch (start us, length us, event | category | flops | bytes accessed | tf_op | source)
XLA Modules:
  0.0 259.9 jit_solution(14394430911966610535)
XLA Ops:
  6.5 0.8 copy.13
  7.5 0.1 reduce_window_sum.11
  7.6 0.2 select_reduce_fusion
  7.8 1.2 broadcast_in_dim.2
  9.0 0.2 reshape.34
  9.2 0.4 convolution_convert_fusion
  9.6 0.5 reshape.35
  10.1 49.6 %all_to_all.25 = bf16[16,5,6144]{2,1,0:T(8,128)(2,1)S(1)} all-to-all(bf16[16,5,6144]{2,1,0:T(8,128)(2,1)S(1)} %reshape.35), channel_id=1, replica_groups=mesh['expert'=16,'fsdp'=16] {'expert'}, dimensions={0} | all-to-all | bytes 1966080 | tf_op jit(solution)/shard_map/all_to_all | solution.py:38
  59.6 1.2 reshape.36
  60.9 107.8 %all-gather.2.cloned.1.call-done = bf16[1280,6144]{1,0:T(8,128)(2,1)} async-done(((bf16[80,6144]{1,0:T(8,128)(2,1)}), bf16[1280,6144]{1,0:T(8,128)(2,1)}) %all-gather.2.cloned.1.call-update) | async-done | bytes 15728656 | tf_op jit(solution)/shard_map/all_gather | solution.py:40
  168.7 11.7 %fusion.3 = f32[1280,336]{0,1:T(8,128)S(1)} fusion(bf16[1280,6144]{1,0:T(8,128)(2,1)} %all-gather.2.cloned.1.call-done, bf16[1,336,6144]{2,1,0:T(8,128)(2,1)} %param.8), kind=kOutput, calls=%fused_computation.5 | convolution fusion | flops 5284823040 | bytes 21577728 | tf_op jit(solution)/shard_map/dot_general | solution.py:8
  180.5 0.5 copy-done.2
  181.0 8.9 %fusion.8 = bf16[1280,336]{0,1:T(8,128)(2,1)S(1)} fusion(bf16[1280,6144]{1,0:T(8,128)(2,1)S(1)} %copy-done.1, bf16[1,336,6144]{2,1,0:T(8,128)(2,1)S(1)} %copy-done.2, f32[1280,336]{0,1:T(8,128)S(1)} %fusion.3), kind=kOutput, calls=%fused_computation.8 | convolution fusion | flops 5313208320 | bytes 22437888 | tf_op jit(solution)/shard_map/dot_general | solution.py:11
  190.0 0.6 copy.14
  190.6 0.7 reshape.37
  191.3 0.7 copy.15
  192.0 34.7 %all_to_all.26 = bf16[16,16,5,336]{3,0,2,1:T(8,128)(2,1)S(1)} all-to-all(bf16[16,16,5,336]{3,0,2,1:T(8,128)(2,1)S(1)} %copy.15), channel_id=1, replica_groups=mesh['expert'=16,'fsdp'=16] {'expert'}, dimensions={1} | all-to-all | bytes 1720320 | tf_op jit(solution)/shard_map/all_to_all | solution.py:45
  226.7 1.2 copy.16
  227.8 5.0 %all-to-all-start.2 = ((bf16[16,16,5,336]{3,1,2,0:T(8,128)(2,1)}), bf16[16,16,5,336]{3,1,2,0:T(8,128)(2,1)S(1)}, u32[]{:S(2)}, u32[]{:S(2)}) async-start(bf16[16,16,5,336]{3,1,2,0:T(8,128)(2,1)} %copy.16), calls=%async_computation.2 | async-start | bytes 1966080 | tf_op jit(solution)/shard_map/all_to_all | solution.py:46
  233.0 17.3 %all-to-all-done.2 = bf16[16,16,5,336]{3,1,2,0:T(8,128)(2,1)S(1)} async-done(((bf16[16,16,5,336]{3,1,2,0:T(8,128)(2,1)}), bf16[16,16,5,336]{3,1,2,0:T(8,128)(2,1)S(1)}, u32[]{:S(2)}, u32[]{:S(2)}) %all-to-all-start.2) | async-done | bytes 860192 | tf_op jit(solution)/shard_map/all_to_all | solution.py:46
  250.3 0.2 copy.17
  250.5 1.2 reshape.38
  251.7 0.4 fusion
  252.1 1.0 reshape.39
  (12 shorter events, 0.4 us)
Async XLA Ops:
  6.5 162.2 %all-gather.2.cloned.1.call-start = ((), (), s32[]{:S(2)}) async-start(), calls=%async_computation.3 | async-start | bytes 16711680 | tf_op jit(solution)/shard_map/all_gather | solution.py:40
  168.7 11.8 %copy-start.1 = (bf16[1280,6144]{1,0:T(8,128)(2,1)S(1)}, bf16[1280,6144]{1,0:T(8,128)(2,1)}, u32[]{:S(2)}) copy-start(bf16[1280,6144]{1,0:T(8,128)(2,1)} %all-gather.2.cloned.1.call-done) | copy-start | bytes 47185924
  168.7 12.3 %copy-start.2 = (bf16[1,336,6144]{2,1,0:T(8,128)(2,1)S(1)}, bf16[1,336,6144]{2,1,0:T(8,128)(2,1)}, u32[]{:S(2)}) copy-start(bf16[1,336,6144]{2,1,0:T(8,128)(2,1)} %param.9) | copy-start | bytes 12386308
  226.7 6.2 %copy-start = (f32[16,4]{0,1:T(4,128)S(1)}, f32[16,4]{0,1:T(4,128)}, u32[]{:S(2)}) copy-start(f32[16,4]{0,1:T(4,128)} %param.7) | copy-start | bytes 772
  227.8 22.5 %all-to-all-start.2 = ((bf16[16,16,5,336]{3,1,2,0:T(8,128)(2,1)}), bf16[16,16,5,336]{3,1,2,0:T(8,128)(2,1)S(1)}, u32[]{:S(2)}, u32[]{:S(2)}) async-start(bf16[16,16,5,336]{3,1,2,0:T(8,128)(2,1)} %copy.16), calls=%async_computation.2 | async-start | bytes 1966080 | tf_op jit(solution)/shard_map/all_to_all | solution.py:46
Sparse Core Ops, SparseCore 0:
  61.0 107.6 all-gather.1
where the time goes:
time: 260 us
  waiting for transfers between devices  125 us (48%)
  blocking collectives  84.3 us (32%)
  matrix products  21.5 us (8%)
  between operations  13.5 us (5%)
  local copies, waits for them, and re-layouts  10.2 us (4%)
  starting transfers between devices  4.97 us (2%)
    all_gather x1, waiting for transfers between devices, local(): lax.all_gather(arrived.reshape(-1, model_width), 'fsdp', axis=0, tiled=True)  108 us
    all_to_all x1, blocking collectives, local(): lax.all_to_all(outgoing, 'expert', split_axis=0, concat_axis=0, tiled=True)  49.6 us
    all_to_all x1, blocking collectives, local(): lax.all_to_all(shaped, 'expert', split_axis=1, concat_axis=1, tiled=True)  34.7 us
    all_to_all x1, waiting for transfers between devices, local(): lax.all_to_all(step_one, 'fsdp', split_axis=0, concat_axis=3, tiled=True)  17.3 us
    dot_general x1, matrix products, hidden_block(): lax.dot_general(row_block, gate_rows, (((1,), (1,)), ((), ())), preferred...  11.7 us
    dot_general x1, matrix products, hidden_block(): lax.dot_general(row_block, up_rows, (((1,), (1,)), ((), ())), preferred_e...  8.93 us
  transfers between devices with their start and end apart: 2, of which 2 were waited for; matrix products, arithmetic and copies ran while one was open for 0% of the time, Pallas kernels for 0%

commit v1 on v0

--- a/solution.py
+++ b/solution.py
@@ -2,6 +2,13 @@
 import jax.numpy as jnp
 from jax import lax
 from jax.sharding import PartitionSpec as P
+
+
+def exchange_gather(value, axis, dim):
+    devices = lax.axis_size(axis)
+    tiles = jnp.stack([value for _ in range(devices)])
+    tiles = lax.all_to_all(tiles, axis, split_axis=0, concat_axis=0)
+    return jnp.concatenate(tiles, axis=dim)
 
 
 def hidden_block(row_block, gate_rows, up_rows):
@@ -37,9 +44,7 @@
     columns = gate_rows.shape[0]
     arrived = lax.all_to_all(outgoing, "expert", split_axis=0, concat_axis=0, tiled=True)
     local_hidden = hidden_block(
-        lax.all_gather(arrived.reshape(-1, model_width), "fsdp", axis=0, tiled=True),
-        gate_rows,
-        up_rows,
+        exchange_gather(arrived.reshape(-1, model_width), "fsdp", 0), gate_rows, up_rows
     )
     shaped = local_hidden.reshape(fsdp_size, experts, cap_slots, columns)
     step_one = lax.all_to_all(shaped, "expert", split_axis=1, concat_axis=1, tiled=True)

time: 260 us -> 316 us (1.22)
  blocking collectives: 84.3 us -> 261 us
  waiting for transfers between devices: 125 us -> 17.3 us
  between operations: 13.5 us -> 0.15 us
    all_to_all x0 -> x1, blocking collectives: none -> 181 us  [exchange_gather(): tiles = lax.all_to_all(tiles, axis, split_axis=0, concat_axis=0)]
    all_gather x1 -> x0, waiting for transfers between devices: 108 us -> none  [local(): lax.all_gather(arrived.reshape(-1, model_width), 'fsdp', axis=0, tiled=True)]
    dot_general x1, matrix products: 8.93 us -> 15.7 us  [hidden_block(): lax.dot_general(row_block, up_rows, (((1,), (1,)), ((), ())), preferred_e...]
    dot_general x1, matrix products: 11.7 us -> 5.58 us  [hidden_block(): lax.dot_general(row_block, gate_rows, (((1,), (1,)), ((), ())), preferred...]
    all_to_all x1, blocking collectives: 34.7 us -> 30.6 us  [local(): lax.all_to_all(shaped, 'expert', split_axis=1, concat_axis=1, tiled=True)]
  transfers between devices with their start and end apart: 2 -> 1, of which waited for: 2 -> 1; matrix products, arithmetic and copies ran while one was open for 0% -> 0% of each run, Pallas kernels for 0% -> 0%
where the time goes in v1:
time: 316 us
  blocking collectives  261 us (83%)
  matrix products  22.1 us (7%)
  waiting for transfers between devices  17.3 us (5%)
  local copies, waits for them, and re-layouts  10.7 us (3%)
  starting transfers between devices  3.72 us (1%)
    all_to_all x1, blocking collectives, exchange_gather(): tiles = lax.all_to_all(tiles, axis, split_axis=0, concat_axis=0)  181 us
    all_to_all x1, blocking collectives, local(): lax.all_to_all(outgoing, 'expert', split_axis=0, concat_axis=0, tiled=True)  49.6 us
    all_to_all x1, blocking collectives, local(): lax.all_to_all(shaped, 'expert', split_axis=1, concat_axis=1, tiled=True)  30.6 us
    all_to_all x1, waiting for transfers between devices, local(): lax.all_to_all(step_one, 'fsdp', split_axis=0, concat_axis=3, tiled=True)  17.3 us
    dot_general x1, matrix products, hidden_block(): lax.dot_general(row_block, up_rows, (((1,), (1,)), ((), ())), preferred_e...  15.7 us
  transfers between devices with their start and end apart: 1, of which 1 were waited for; matrix products, arithmetic and copies ran while one was open for 0% of the time, Pallas kernels for 0%

profile of v1, /device:TPU:1, one launch (start us, length us, event | category | flops | bytes accessed | tf_op | source)
XLA Modules:
  0.0 315.5 jit_solution(16552657904555648732)
XLA Ops:
  0.0 0.8 copy.13
  0.9 0.1 reduce_window_sum.11
  1.0 0.2 select_reduce_fusion
  1.2 1.2 broadcast_in_dim.2
  2.5 0.2 reshape.36
  2.6 0.4 convolution_convert_fusion
  3.0 0.5 reshape.37
  3.5 49.6 %all_to_all.30 = bf16[16,5,6144]{2,1,0:T(8,128)(2,1)S(1)} all-to-all(bf16[16,5,6144]{2,1,0:T(8,128)(2,1)S(1)} %reshape.37), channel_id=1, replica_groups=mesh['expert'=16,'fsdp'=16] {'expert'}, dimensions={0} | all-to-all | bytes 1966080 | tf_op jit(solution)/shard_map/all_to_all | solution.py:45
  53.1 0.5 stack_reshape.2
  53.6 2.0 stack.3
  55.6 181.0 %all_to_all.31 = bf16[16,80,6144]{2,1,0:T(8,128)(2,1)S(1)} all-to-all(bf16[16,80,6144]{2,1,0:T(8,128)(2,1)S(1)} %stack.3), channel_id=1, replica_groups=mesh['expert'=16,'fsdp'=16] {'fsdp'}, dimensions={0} | all-to-all | bytes 31457280 | tf_op jit(solution)/shard_map/all_to_all | solution.py:10
  236.6 5.6 %fusion.3 = f32[1280,336]{0,1:T(8,128)S(1)} fusion(bf16[1280,6144]{1,0:T(8,128)(2,1)S(1)} %bitcast.20, bf16[1,336,6144]{2,1,0:T(8,128)(2,1)S(1)} %copy-done.1), kind=kOutput, calls=%fused_computation.5 | convolution fusion | flops 5284823040 | bytes 21577728 | tf_op jit(solution)/shard_map/dot_general | solution.py:15
  242.2 15.7 %fusion.8 = bf16[1280,336]{0,1:T(8,128)(2,1)S(1)} fusion(bf16[1280,6144]{1,0:T(8,128)(2,1)S(1)} %bitcast.21, bf16[1,336,6144]{2,1,0:T(8,128)(2,1)} %param.9, f32[1280,336]{0,1:T(8,128)S(1)} %fusion.3), kind=kOutput, calls=%fused_computation.8 | convolution fusion | flops 5313208320 | bytes 22437888 | tf_op jit(solution)/shard_map/dot_general | solution.py:18
  258.0 0.6 copy.14
  258.6 0.5 reshape.39
  259.1 0.7 copy.15
  259.8 30.6 %all_to_all.32 = bf16[16,16,5,336]{3,0,2,1:T(8,128)(2,1)S(1)} all-to-all(bf16[16,16,5,336]{3,0,2,1:T(8,128)(2,1)S(1)} %copy.15), channel_id=1, replica_groups=mesh['expert'=16,'fsdp'=16] {'expert'}, dimensions={1} | all-to-all | bytes 1720320 | tf_op jit(solution)/shard_map/all_to_all | solution.py:50
  290.4 1.2 copy.16
  291.5 3.7 %all-to-all-start.3 = ((bf16[16,16,5,336]{3,1,2,0:T(8,128)(2,1)}), bf16[16,16,5,336]{3,1,2,0:T(8,128)(2,1)S(1)}, u32[]{:S(2)}, u32[]{:S(2)}) async-start(bf16[16,16,5,336]{3,1,2,0:T(8,128)(2,1)} %copy.16), calls=%async_computation.3 | async-start | bytes 1966080 | tf_op jit(solution)/shard_map/all_to_all | solution.py:51
  295.4 17.3 %all-to-all-done.3 = bf16[16,16,5,336]{3,1,2,0:T(8,128)(2,1)S(1)} async-done(((bf16[16,16,5,336]{3,1,2,0:T(8,128)(2,1)}), bf16[16,16,5,336]{3,1,2,0:T(8,128)(2,1)S(1)}, u32[]{:S(2)}, u32[]{:S(2)}) %all-to-all-start.3) | async-done | bytes 860192 | tf_op jit(solution)/shard_map/all_to_all | solution.py:51
  312.7 0.2 copy.17
  312.9 1.2 reshape.40
  314.1 0.4 fusion
  314.5 1.0 reshape.41
  (9 shorter events, 0.3 us)
Async XLA Ops:
  55.6 181.0 %copy-start.1 = (bf16[1,336,6144]{2,1,0:T(8,128)(2,1)S(1)}, bf16[1,336,6144]{2,1,0:T(8,128)(2,1)}, u32[]{:S(2)}) copy-start(bf16[1,336,6144]{2,1,0:T(8,128)(2,1)} %param.8) | copy-start | bytes 12386308
  290.4 4.9 %copy-start = (f32[16,4]{0,1:T(4,128)S(1)}, f32[16,4]{0,1:T(4,128)}, u32[]{:S(2)}) copy-start(f32[16,4]{0,1:T(4,128)} %param.7) | copy-start | bytes 772
  291.5 21.2 %all-to-all-start.3 = ((bf16[16,16,5,336]{3,1,2,0:T(8,128)(2,1)}), bf16[16,16,5,336]{3,1,2,0:T(8,128)(2,1)S(1)}, u32[]{:S(2)}, u32[]{:S(2)}) async-start(bf16[16,16,5,336]{3,1,2,0:T(8,128)(2,1)} %copy.16), calls=%async_computation.3 | async-start | bytes 1966080 | tf_op jit(solution)/shard_map/all_to_all | solution.py:51
